TPU v7x, 32 devices: a whole 2x2x4 slice. The times are simulated.
32 devices in a mesh: seq: 8 (over z, y), exp: 4 (over x, core).
Axes of the slice: x: 2, y: 2, z: 4, core: 2. Of those that a mesh axis runs over, the one named last changes fastest.
Arguments:
- hidden: bfloat16 [4, 1024, 2048], P('exp', 'seq'), may hold values from -6 to 6
- lengths: int32 [4, 4], P('exp'), may hold values from 1 to 512, 1024 in all within a row
- attn_gain: float32 [2048], replicated, may hold values from 0 to 10
- w_qkv: bfloat16 [2048, 3, 16, 128], P(None, None, 'seq'), may hold values from -0.125 to 0.125
- w_out: bfloat16 [16, 128, 2048], P('seq'), may hold values from -0.125 to 0.125
- moe_gain: float32 [2048], replicated, may hold values from 0.5 to 1.5
- router: bfloat16 [2048, 16], replicated, may hold values from -8 to 8
- routes: int32 [4, 1024, 6], P('exp', 'seq'), may hold values from 0 to 15, all different within a row; in each aligned block of 128 rows (0 to 127, 128 to 255, ..., all dimensions but the last counted through in order) at most 56 rows name the same one
- w_gate_up: bfloat16 [32, 2, 704, 2048], P(('seq', 'exp')), may hold values from -0.125 to 0.125
- w_down: bfloat16 [32, 704, 2048], P(('seq', 'exp')), may hold values from -0.15625 to 0.15625
- final_gain: float32 [2048], replicated, may hold values from 0.5 to 1.5
- lm_head: bfloat16 [102400, 2048], P(('seq', 'exp')), may hold values from -4 to 4
Outputs:
- layer_out: bfloat16 [4, 1024, 2048], P('exp', 'seq')
- logprobs: float32 [16, 102400], P(None, ('seq', 'exp'))
Inputs may be any that keep to these rules, and one draw needn't show every extreme that they name: `routes`: in the rows of one device no expert is named by more than 56 rows; in some devices one expert is named by exactly 56 rows. `lengths`: each row sums to 1024; its largest entry is 512.
All inputs are finite; a program needn't handle non-finite values.
Results may differ from a plain program's by a relative error of at most 0.0095.
The roundings to bfloat16 on the way count: a program that leaves them out, or rounds other values in their place, can miss the bound.
Values may be sent and summed in bfloat16 or wider, within the bound.
No kernel may reach another device: no remote copies, remote signals or barrier semaphores. Data moves between devices by JAX's collectives and lax.ppermute only.
A program may use at most 128 MiB of HBM per device.

v0:
```python
import jax
import jax.numpy as jnp
from jax import lax
from jax.sharding import PartitionSpec as P

epsilon = 1e-06


def joined(value, axis, join):
    pieces = jax.tree.map(lambda part: lax.all_gather(part, axis), value)
    head = jax.tree.map(lambda part: part[0], pieces)
    tail = jax.tree.map(lambda part: part[1:], pieces)
    subtotal, _ = lax.scan(lambda subtotal, piece: (join(subtotal, piece), None), head, tail)
    return subtotal


def rms_scale(values, gain):
    widened = values.astype(jnp.float32)
    inverse = lax.rsqrt(jnp.mean(widened * widened, axis=-1, keepdims=True) + epsilon)
    return widened * inverse * gain


def segment_layout(prompt_lengths, count):
    ends = jnp.cumsum(prompt_lengths)
    starts = ends - prompt_lengths
    places = jnp.arange(count, dtype=jnp.int32)
    member = ((places[:, None] >= starts[None, :]) & (places[:, None] < ends[None, :])).astype(
        jnp.int32
    )
    numbers = jnp.arange(prompt_lengths.shape[0], dtype=jnp.int32)
    segment = jnp.sum(member * numbers[None, :], axis=1)
    offset = places - jnp.sum(member * starts[None, :], axis=1)
    return (segment, offset)


def rotary(values, positions):
    half_size = values.shape[-1] // 2
    freqs = 10000.0 ** (-2.0 * jnp.arange(half_size, dtype=jnp.float32) / values.shape[-1])
    angles = positions.astype(jnp.float32)[:, None] * freqs[None, :]
    cosine = jnp.cos(angles)[:, None, :]
    sine = jnp.sin(angles)[:, None, :]
    first_half = values[..., :half_size]
    second_half = values[..., half_size:]
    return jnp.concatenate(
        [first_half * cosine - second_half * sine, second_half * cosine + first_half * sine],
        axis=-1,
    )


def pair_swap(value):
    count = lax.axis_size("exp")
    return lax.ppermute(value, "exp", [(i, i ^ 1) for i in range(count)])


def merge_softmax(earlier, later):
    highest = jnp.maximum(earlier[0], later[0])
    return (
        highest,
        earlier[1] * jnp.exp(earlier[0] - highest) + later[1] * jnp.exp(later[0] - highest),
    )


def per_device(
    hidden,
    lengths,
    attn_gain,
    w_qkv,
    w_out,
    moe_gain,
    router,
    routes,
    w_gate_up,
    w_down,
    final_gain,
    lm_head,
):
    seq_count = lax.axis_size("seq")
    group_count = lax.axis_size("exp")
    device_count = seq_count * group_count
    token_rows = hidden[0]
    tok_rows = token_rows.shape[0]
    model_width = token_rows.shape[1]
    group_tokens = tok_rows * seq_count
    head_count = w_qkv.shape[2]
    head_size = w_qkv.shape[3]
    scale_factor = head_size ** (-0.5)
    prompt_lengths = lengths[0]
    segment, offset = segment_layout(prompt_lengths, group_tokens)
    normed = rms_scale(token_rows, attn_gain).astype(jnp.bfloat16)
    qkv_weight = w_qkv.reshape(model_width, 3 * head_count * head_size)
    qkv = jnp.dot(
        lax.all_gather(normed, "seq", axis=0, tiled=True),
        qkv_weight,
        preferred_element_type=jnp.float32,
    ).reshape(group_tokens, 3, head_count, head_size)
    query = rotary(qkv[:, 0], offset).astype(jnp.bfloat16)
    keys = rotary(qkv[:, 1], offset).astype(jnp.bfloat16)
    values = qkv[:, 2].astype(jnp.bfloat16)
    block_rows = min(512, group_tokens)
    key_places = jnp.arange(group_tokens, dtype=jnp.int32)

    def one_block(block_index):
        first_row = block_index * block_rows
        block_query = lax.dynamic_slice_in_dim(query, first_row, block_rows, 0)
        block_segment = lax.dynamic_slice_in_dim(segment, first_row, block_rows, 0)
        query_places = first_row + jnp.arange(block_rows, dtype=jnp.int32)
        scores = (
            jnp.einsum("qhd,khd->hqk", block_query, keys, preferred_element_type=jnp.float32)
            * scale_factor
        )
        allowed = (block_segment[:, None] == segment[None, :]) & (
            key_places[None, :] <= query_places[:, None]
        )
        scores = jnp.where(allowed[None], scores, -1e30)
        highest = jnp.max(scores, axis=2, keepdims=True)
        weights = jnp.exp(scores - highest)
        probs = (weights / jnp.sum(weights, axis=2, keepdims=True)).astype(jnp.bfloat16)
        return jnp.einsum("hqk,khd->qhd", probs, values, preferred_element_type=jnp.float32).astype(
            jnp.bfloat16
        )

    blocks = lax.map(one_block, jnp.arange(group_tokens // block_rows, dtype=jnp.int32))
    heads_flat = blocks.reshape(group_tokens, head_count * head_size)
    regrouped = lax.all_to_all(heads_flat, "seq", split_axis=0, concat_axis=1, tiled=True)
    core = lax.axis_index("exp") % 2
    half_size = head_size // 2
    own_half = lax.dynamic_slice_in_dim(w_out, core * half_size, half_size, axis=1)
    own_weight = lax.all_gather(own_half, "seq", axis=0, tiled=True)
    other_weight = pair_swap(own_weight)
    regrouped = regrouped.reshape(tok_rows, -1, head_size)
    own_heads = lax.dynamic_slice_in_dim(regrouped, core * half_size, half_size, axis=2)
    other_heads = lax.dynamic_slice_in_dim(regrouped, (1 - core) * half_size, half_size, axis=2)
    mixed = jnp.einsum(
        "thd,hdo->to", own_heads, own_weight, preferred_element_type=jnp.float32
    ) + jnp.einsum("thd,hdo->to", other_heads, other_weight, preferred_element_type=jnp.float32)
    middle = (token_rows.astype(jnp.float32) + mixed).astype(jnp.bfloat16)
    expert_in = rms_scale(middle, moe_gain).astype(jnp.bfloat16)
    logits = jnp.dot(expert_in, router, preferred_element_type=jnp.float32)
    expert_count = router.shape[1]
    token_routes = routes[0]
    top_count = token_routes.shape[1]
    expert_ids = jnp.arange(expert_count, dtype=jnp.int32)
    chosen_mask = token_routes[:, :, None] == expert_ids[None, None, :]
    chosen = jnp.sum(jnp.where(chosen_mask, logits[:, None, :], 0.0), axis=2)
    gates = jax.nn.softmax(chosen, axis=-1)
    capacity = max(2, tok_rows * top_count * 7 // (6 * expert_count))
    flat_mask = chosen_mask.reshape(tok_rows * top_count, expert_count).astype(jnp.int32)
    earlier_count = jnp.cumsum(flat_mask, axis=0) - flat_mask
    slot_index = jnp.sum(earlier_count * flat_mask, axis=1)
    target = (token_routes.reshape(-1) * capacity + slot_index).reshape(tok_rows, top_count)
    slot_total = expert_count * capacity
    placed = target[:, :, None] == jnp.arange(slot_total, dtype=jnp.int32)[None, None, :]
    dispatch_table = jnp.any(placed, axis=1).astype(jnp.bfloat16)
    slot_weights = jnp.sum(jnp.where(placed, gates[:, :, None], 0.0), axis=1)
    packed = lax.dot_general(
        dispatch_table, expert_in, (((0,), (0,)), ((), ())), preferred_element_type=jnp.float32
    ).astype(jnp.bfloat16)
    shares = device_count // expert_count
    assert capacity % shares == 0
    outgoing = packed.reshape(device_count, capacity // shares, model_width)
    gate_up = w_gate_up[0]
    down_weight = w_down[0]
    other_gate_up = pair_swap(gate_up)
    other_down = pair_swap(down_weight)
    arrived = lax.all_to_all(outgoing, ("seq", "exp"), split_axis=0, concat_axis=0, tiled=True)
    arrived_shape = arrived.shape
    flat_rows = arrived.reshape(-1, model_width)

    def share_part(pair, down):
        both = jnp.einsum("rd,gfd->rgf", flat_rows, pair, preferred_element_type=jnp.float32)
        act = (jax.nn.silu(both[:, 0]) * both[:, 1]).astype(jnp.bfloat16)
        part = jnp.dot(act, down, preferred_element_type=jnp.float32).astype(jnp.bfloat16)
        return part.astype(jnp.float32)

    part_sum = share_part(gate_up, down_weight) + share_part(other_gate_up, other_down)
    returned = lax.all_to_all(
        part_sum.astype(jnp.bfloat16).reshape(arrived_shape),
        ("seq", "exp"),
        split_axis=0,
        concat_axis=0,
        tiled=True,
    )
    summed = returned.reshape(slot_total, model_width).astype(jnp.float32)
    routed = jnp.dot(
        slot_weights, summed, precision=lax.Precision.HIGHEST, preferred_element_type=jnp.float32
    )
    layer_rows = (middle.astype(jnp.float32) + routed).astype(jnp.bfloat16)
    prompt_count = prompt_lengths.shape[0]
    last_places = jnp.cumsum(prompt_lengths) - 1
    here_places = lax.axis_index("seq") * tok_rows + jnp.arange(tok_rows, dtype=jnp.int32)
    select_table = (last_places[:, None] == here_places[None, :]).astype(jnp.bfloat16)
    picked = jnp.dot(select_table, layer_rows, preferred_element_type=jnp.float32)
    board = jnp.zeros((group_count * prompt_count, model_width), jnp.bfloat16)
    board = lax.dynamic_update_slice_in_dim(
        board, picked.astype(jnp.bfloat16), lax.axis_index("exp") * prompt_count, 0
    )
    last_rows = lax.psum(board, ("seq", "exp")).astype(jnp.float32)
    final = rms_scale(last_rows, final_gain).astype(jnp.bfloat16)
    vocab_scores = lax.dot_general(
        final, lm_head, (((1,), (1,)), ((), ())), preferred_element_type=jnp.float32
    )
    local_peak = jnp.max(vocab_scores, axis=1)
    local_total = jnp.sum(jnp.exp(vocab_scores - local_peak[:, None]), axis=1)
    global_peak, global_total = joined((local_peak, local_total), ("seq", "exp"), merge_softmax)
    logprobs = vocab_scores - (global_peak + jnp.log(global_total))[:, None]
    return (layer_rows[None], logprobs)


def solution(mesh):
    return jax.shard_map(
        per_device,
        mesh=mesh,
        in_specs=(
            P("exp", "seq", None),
            P("exp", None),
            P(),
            P(None, None, "seq", None),
            P("seq", None, None),
            P(),
            P(),
            P("exp", "seq", None),
            P(("seq", "exp"), None, None, None),
            P(("seq", "exp"), None, None),
            P(),
            P(("seq", "exp"), None),
        ),
        out_specs=(P("exp", "seq", None), P(None, ("seq", "exp"))),
        check_vma=False,
    )
```

profile of v0, /device:TPU:0, one launch (start us, length us, event | category | flops | bytes accessed | tf_op | source)
XLA Modules:
  0.0 637.5 jit_solution(17529622819611426284)
XLA Ops:
  7.2 1.3 fusion.48
  8.6 2.1 fusion.50
  10.7 0.8 constant_dynamic-slice_fusion.2
  11.8 8.0 %reshape.269 = bf16[2048,768]{1,0:T(8,128)(2,1)} reshape(bf16[2048,3,2,128]{3,2,1,0:T(2,128)(2,1)} %param.19) | data formatting | bytes 6291456 | tf_op jit(solution)/shard_map/reshape | solution.py:90
  19.8 4.8 copy.43
  24.7 1.0 multiply_cosine_fusion
  25.7 61.2 %all-gather.5.cloned.1.call-done = bf16[1024,2048]{1,0:T(8,128)(2,1)} async-done(((bf16[128,2048]{1,0:T(8,128)(2,1)}), bf16[1024,2048]{1,0:T(8,128)(2,1)}) %all-gather.5.cloned.1.call-update) | async-done | bytes 4194320 | tf_op jit(solution)/shard_map/all_gather | solution.py:92
  86.9 6.2 fusion.31
  93.6 1.2 copy-done.4
  95.2 1.4 fusion.51
  96.8 64.4 %all-gather.7.cloned.1.call-done = bf16[16,64,2048]{2,1,0:T(8,128)(2,1)} async-done(((bf16[2,64,2048]{2,1,0:T(8,128)(2,1)}), bf16[16,64,2048]{2,1,0:T(8,128)(2,1)}) %all-gather.7.cloned.1.call-update) | async-done | bytes 4194320 | tf_op jit(solution)/shard_map/all_gather | solution.py:128
  161.3 17.8 %while.24 = (s32[]{:T(128)}, bf16[2,512,2,128]{3,2,1,0:T(2,128)(2,1)S(1)}, s32[2]{0:T(128)S(1)}, s32[1024]{0:T(1024)S(1)}, bf16[1024,2,128]{0,2,1:T(8,128)(2,1)S...) while((s32[]{:T(128)}, ...), condition=%wide.region_7.8_spmd.clone, body=%wide.region_4.7_spmd.clone.sunk | while | flops 544867840 | bytes 11557047 | solution.py:122
  161.3 0.6 dynamic_slice.72
  162.6 0.6 fusion.116
  163.2 3.7 fusion.117
  166.9 2.9 fusion.118
  170.2 0.6 dynamic_slice.72
  171.5 0.6 fusion.116
  172.1 3.7 fusion.117
  175.8 2.9 fusion.118
  179.1 1.1 all_to_all.18
  180.2 3.7 all-to-all-start
  184.3 1.7 reduce-window.11
  186.7 0.5 fusion.33
  187.1 12.0 %all-to-all-done = bf16[8,128,256]{2,1,0:T(8,128)(2,1)S(1)} async-done(((bf16[8,128,256]{2,1,0:T(8,128)(2,1)}), bf16[8,128,256]{2,1,0:T(8,128)(2,1)S(1)}, u32[]{:S(2)}, u32[]{:S(2)}) %all-to-all-start) | async-done | bytes 524320 | tf_op jit(solution)/shard_map/all_to_all | solution.py:124
  199.4 2.9 convolution_bitcast_fusion.1
  202.4 3.1 multiply_reduce_fusion
  205.5 3.0 convolution_convert_fusion
  208.5 5.8 reshape.272
  214.3 3.7 all-to-all-start.1
  218.6 93.3 %all-to-all-done.1 = bf16[32,28,2048]{2,1,0:T(8,128)(2,1)} async-done(((bf16[32,28,2048]{2,1,0:T(8,128)(2,1)}), bf16[32,28,2048]{2,1,0:T(8,128)(2,1)}, u32[]{:S(2)}, u32[]{:S(2)}) %all-to-all-start.1) | async-done | bytes 3670048 | tf_op jit(solution)/shard_map/all_to_all | solution.py:165
  311.9 5.9 reshape.292
  317.8 9.4 %fusion.76 = f32[896,2,704]{0,2,1:T(8,128)S(1)} fusion(bf16[896,2048,1]{1,0,2:T(8,128)(2,1)} %reshape.292, bf16[1,2,704,2048]{3,2,1,0:T(8,128)(2,1)} %param.24), kind=kOutput, calls=%fused_computation.127 | convolution fusion | flops 5167382528 | bytes 14483456 | tf_op jit(solution)/shard_map/rd,gfd->rgf/dot_general | solution.py:170
  327.3 3.4 fusion.44
  330.7 8.4 %fusion.88 = f32[896,2,704]{0,2,1:T(8,128)S(1)} fusion(bf16[896,2048,1]{1,0,2:T(8,128)(2,1)S(1)} %copy-done.3, bf16[2,704,2048]{2,1,0:T(8,128)(2,1)} %collective-permute-done.1), kind=kOutput, calls=%fused_computation.134 | convolution fusion | flops 5167382528 | bytes 14483456 | tf_op jit(solution)/shard_map/rd,gfd->rgf/dot_general | solution.py:170
  339.2 6.9 %add_convert_fusion = bf16[896,2048]{1,0:T(8,128)(2,1)} fusion(bf16[896,2048]{1,0:T(8,128)(2,1)S(1)} %fusion.44, bf16[704,2048]{1,0:T(8,128)(2,1)} %collective-permute-done.2, f32[896,2,704]{0,2,1:T(8,128)S(1)} %fusion.88), kind=kOutput, calls=%fused_computation.31 | convolution fusion | flops 2596651008 | bytes 15269888 | tf_op jit(solution)/shard_map/dot_general | solution.py:172
  346.0 5.8 reshape.274
  351.9 4.1 all-to-all-start.2
  357.1 92.8 %all-to-all-done.2 = bf16[32,28,2048]{2,1,0:T(8,128)(2,1)} async-done(((bf16[32,28,2048]{2,1,0:T(8,128)(2,1)}), bf16[32,28,2048]{2,1,0:T(8,128)(2,1)}, u32[]{:S(2)}, u32[]{:S(2)}) %all-to-all-start.2) | async-done | bytes 3670048 | tf_op jit(solution)/shard_map/all_to_all | solution.py:176
  449.8 5.8 reshape.275
  455.7 3.9 fusion.40
  459.8 0.6 copy-done.6
  460.5 117.0 %all-reduce.5.cloned.1.call-done = bf16[16,2048]{1,0:T(8,128)(2,1)} async-done(((bf16[16,2048]{1,0:T(8,128)(2,1)}), bf16[16,2048]{1,0:T(8,128)(2,1)}) %all-reduce.5.cloned.1.call-update) | async-done | bytes 65552 | tf_op jit(solution)/shard_map/psum | solution.py:197
  577.5 1.0 fusion.54
  578.5 8.5 %fusion.87 = (f32[16]{0:T(128)S(1)}, f32[16,3200]{1,0:T(8,128)S(1)}) fusion(bf16[3200,2048]{1,0:T(8,128)(2,1)} %param.27, bf16[16,2048]{1,0:T(8,128)(2,1)} %all-reduce.5.cloned.1.call-done, f32[2048]{0:T(1024)S(1)} %copy-done.10, f32[16]{0:T(128)S(1)} %add_rsqrt_fusion), kind=kOutput, calls=%fused_computation.133 | convolution fusion | flops 209897456 | bytes 13385856 | tf_op jit(solution)/shard_map/dot_general | solution.py:199
  587.7 40.8 %all-reduce.2 = (f32[512]{0:T(512)S(1)}, f32[512]{0:T(512)S(1)}) all-reduce(f32[512]{0:T(512)S(1)} %dynamic-update-slice, f32[512]{0:T(512)S(1)} %dynamic-update-slice.1), channel_id=2, replica_groups=mesh['seq'=8,'exp'=4] {'seq','exp'}, use_global_device_ids=true, to_apply=%add | all-reduce | flops 1024 | bytes 8192
  628.8 1.3 while.23
  630.2 0.8 broadcast_subtract_fusion
  (122 shorter events, 7.4 us)
Async XLA Ops:
  7.2 3.5 copy-start
  7.2 4.4 copy-start.12
  7.2 79.7 %all-gather.5.cloned.1.call-start = ((), (), s32[]{:S(2)}) async-start(), calls=%async_computation.3 | async-start | bytes 4718592 | tf_op jit(solution)/shard_map/all_gather | solution.py:92
  10.6 150.7 %all-gather.7.cloned.1.call-start = ((), (), s32[]{:S(2)}) async-start(), calls=%async_computation.4 | async-start | bytes 4718592 | tf_op jit(solution)/shard_map/all_gather | solution.py:128
  93.1 1.7 copy-start.4
  161.3 41.1 %collective-permute-start = (bf16[16,64,2048]{2,1,0:T(8,128)(2,1)}, bf16[16,64,2048]{2,1,0:T(8,128)(2,1)}, u32[]{:S(2)}, u32[]{:S(2)}) collective-permute-start(bf16[16,64,2048]{2,1,0:T(8,128)(2,1)} %all-gather.7.cloned.1.call-done), channel_id=1, source_target_pairs={{0,1},{1,0},{2,3},{3,2},{4,5},{5,4},{6,7},{7,6},{8,9},{9,8},{10,11... | collective-permute-start | bytes 12582920 | tf_op jit(solution)/shard_map/ppermute | solution.py:52
  161.3 22.6 %copy-start.9 = (s32[1,128,6]{1,0,2:T(1,128)S(1)}, s32[1,128,6]{1,0,2:T(1,128)}, u32[]{:S(2)}) copy-start(s32[1,128,6]{1,0,2:T(1,128)} %param.23) | copy-start | bytes 9220
  180.2 18.9 %all-to-all-start = ((bf16[8,128,256]{2,1,0:T(8,128)(2,1)}), bf16[8,128,256]{2,1,0:T(8,128)(2,1)S(1)}, u32[]{:S(2)}, u32[]{:S(2)}) async-start(bf16[8,128,256]{2,1,0:T(8,128)(2,1)} %all_to_all.18), calls=%async_computation | async-start | bytes 1048576 | tf_op jit(solution)/shard_map/all_to_all | solution.py:124
  184.2 18.2 %copy-start.2 = (bf16[1,128,2048]{2,1,0:T(8,128)(2,1)S(1)}, bf16[1,128,2048]{2,1,0:T(8,128)(2,1)}, u32[]{:S(2)}) copy-start(bf16[1,128,2048]{2,1,0:T(8,128)(2,1)} %param.16) | copy-start | bytes 1572868
  202.4 3.1 copy-start.8
  214.3 97.6 %all-to-all-start.1 = ((bf16[32,28,2048]{2,1,0:T(8,128)(2,1)}), bf16[32,28,2048]{2,1,0:T(8,128)(2,1)}, u32[]{:S(2)}, u32[]{:S(2)}) async-start(bf16[32,28,2048]{2,1,0:T(8,128)(2,1)} %reshape.272), calls=%async_computation.1 | async-start | bytes 8388608 | tf_op jit(solution)/shard_map/all_to_all | solution.py:165
  218.1 112.7 %collective-permute-start.1 = (bf16[2,704,2048]{2,1,0:T(8,128)(2,1)}, bf16[2,704,2048]{2,1,0:T(8,128)(2,1)}, u32[]{:S(2)}, u32[]{:S(2)}) collective-permute-start(bf16[2,704,2048]{2,1,0:T(8,128)(2,1)} %bitcast.143), channel_id=1, source_target_pairs={{0,1},{1,0},{2,3},{3,2},{4,5},{5,4},{6,7},{7,6},{8,9},{9,8},{10,11... | collective-permute-start | bytes 17301512 | tf_op jit(solution)/shard_map/ppermute | solution.py:52
  218.3 120.9 %collective-permute-start.2 = (bf16[704,2048]{1,0:T(8,128)(2,1)}, bf16[704,2048]{1,0:T(8,128)(2,1)}, u32[]{:S(2)}, u32[]{:S(2)}) collective-permute-start(bf16[704,2048]{1,0:T(8,128)(2,1)} %bitcast.144), channel_id=1, source_target_pairs={{0,1},{1,0},{2,3},{3,2},{4,5},{5,4},{6,7},{7,6},{8,9},{9,8},{10,11... | collective-permute-start | bytes 8650760 | tf_op jit(solution)/shard_map/ppermute | solution.py:52
  317.8 9.4 %copy-start.11 = (bf16[1,704,2048]{2,1,0:T(8,128)(2,1)S(1)}, bf16[1,704,2048]{2,1,0:T(8,128)(2,1)}, u32[]{:S(2)}) copy-start(bf16[1,704,2048]{2,1,0:T(8,128)(2,1)} %param.25) | copy-start | bytes 8650756
  327.3 3.4 copy-start.3
  351.9 4.4 copy-start.7
  351.9 98.0 %all-to-all-start.2 = ((bf16[32,28,2048]{2,1,0:T(8,128)(2,1)}), bf16[32,28,2048]{2,1,0:T(8,128)(2,1)}, u32[]{:S(2)}, u32[]{:S(2)}) async-start(bf16[32,28,2048]{2,1,0:T(8,128)(2,1)} %reshape.274), calls=%async_computation.2 | async-start | bytes 8388608 | tf_op jit(solution)/shard_map/all_to_all | solution.py:176
  356.0 221.6 %all-reduce.5.cloned.1.call-start = ((), (), s32[]{:S(2)}) async-start(), calls=%async_computation.5 | async-start | bytes 131072 | tf_op jit(solution)/shard_map/psum | solution.py:197
  455.7 122.8 %copy-start.10 = (f32[2048]{0:T(1024)S(1)}, f32[2048]{0:T(1024)}, u32[]{:S(2)}) copy-start(f32[2048]{0:T(1024)} %param.26) | copy-start | bytes 24580
  459.6 127.4 %copy-start.5 = (bf16[128,2048]{1,0:T(8,128)(2,1)}, bf16[128,2048]{1,0:T(8,128)(2,1)S(1)}, u32[]{:S(2)}) copy-start(bf16[128,2048]{1,0:T(8,128)(2,1)S(1)} %fusion.40) | copy-start | bytes 1572868
  459.8 0.6 copy-start.6
  578.5 52.4 %copy-start.1 = (bf16[2,128,2048]{2,1,0:T(8,128)(2,1)S(1)}, bf16[2,128,2048]{2,1,0:T(8,128)(2,1)}, u32[]{:S(2)}) copy-start(bf16[2,128,2048]{2,1,0:T(8,128)(2,1)} %param.20) | copy-start | bytes 3145732
Sparse Core Ops, SparseCore 0:
  10.7 76.0 all-gather.4
  89.6 71.6 all-gather.6
  460.6 116.8 all-reduce.4
where the time goes:
time: 639 us; the launch traced here: 637 us
  waiting for transfers between devices  441 us (69%)
  matrix products  69.6 us (11%)
  local copies, waits for them, and re-layouts  45.9 us (7%)
  blocking collectives  40.8 us (6%)
  between operations  14.3 us (2%)
  starting transfers between devices  12.4 us (2%)
  other arithmetic  11.9 us (2%)
    psum x1, waiting for transfers between devices, per_device(): last_rows = lax.psum(board, ('seq', 'exp')).astype(jnp.float32)  117 us
    all_to_all x1, waiting for transfers between devices, per_device(): lax.all_to_all(outgoing, ('seq', 'exp'), split_axis=0, concat_axis=0, til...  93.3 us
    all_to_all x1, waiting for transfers between devices, per_device(): lax.all_to_all(part_sum.astype(jnp.bfloat16).reshape(arrived_shape), ('se...  92.8 us
    all_gather x1, waiting for transfers between devices, per_device(): own_weight = lax.all_gather(own_half, 'seq', axis=0, tiled=True)  64.4 us
    all_gather x1, waiting for transfers between devices, per_device(): lax.all_gather(normed, 'seq', axis=0, tiled=True)  61.2 us
    unnamed x1, blocking collectives  40.8 us
    dot_general x2, matrix products, share_part(): jnp.einsum('rd,gfd->rgf', flat_rows, pair, preferred_element_type=jnp.flo...  17.8 us
  transfers between devices with their start and end apart: 9, of which 6 were waited for; matrix products, arithmetic and copies ran while one was open for 12% of the time, Pallas kernels for 0%

commit v1 on v0

--- a/solution.py
+++ b/solution.py
@@ -4,6 +4,17 @@
 from jax.sharding import PartitionSpec as P
 
 epsilon = 1e-06
+
+
+def split_up(x, dim, length):
+    before, after = (x.shape[:dim], x.shape[dim + 1 :])
+    return jnp.moveaxis(x.reshape(*before, length, -1, *after), dim, 0)
+
+
+def joined_along(parts, dim):
+    parts = jnp.moveaxis(parts, 0, dim)
+    dims = parts.shape
+    return parts.reshape(*dims[:dim], dims[dim] * dims[dim + 1], *dims[dim + 2 :])
 
 
 def joined(value, axis, join):
@@ -121,7 +132,14 @@
 
     blocks = lax.map(one_block, jnp.arange(group_tokens // block_rows, dtype=jnp.int32))
     heads_flat = blocks.reshape(group_tokens, head_count * head_size)
-    regrouped = lax.all_to_all(heads_flat, "seq", split_axis=0, concat_axis=1, tiled=True)
+    size, place = (lax.axis_size("seq"), lax.axis_index("seq"))
+    parts = split_up(heads_flat, 0, size)
+    outs = [parts[place]]
+    for step in range(1, size):
+        sent = parts[place ^ step]
+        outs.append(lax.ppermute(sent, "seq", [(i_2, i_2 ^ step) for i_2 in range(size)]))
+    parts = jnp.stack(outs)[place ^ jnp.arange(size)]
+    regrouped = joined_along(parts, 1)
     core = lax.axis_index("exp") % 2
     half_size = head_size // 2
     own_half = lax.dynamic_slice_in_dim(w_out, core * half_size, half_size, axis=1)

time: 639 us -> 638 us (level)
  waiting for transfers between devices: 441 us -> 430 us
  starting transfers between devices: 12.4 us -> 21.7 us
    all_to_all x1 -> x0, waiting for transfers between devices: 12 us -> none  [per_device(): lax.all_to_all(heads_flat, 'seq', split_axis=0, concat_axis=1, tiled=True)]
    ppermute x0 -> x7, starting transfers between devices: none -> 11.3 us  [per_device(): lax.ppermute(sent, 'seq', [(i_2, i_2 ^ step) for i_2 in range(size)])]
  transfers between devices with their start and end apart: 9 -> 15, of which waited for: 6 -> 7; matrix products, arithmetic and copies ran while one was open for 12% -> 12% of each run, Pallas kernels for 0% -> 0%
where the time goes in v1:
time: 638 us; the launch traced here: 636 us
  waiting for transfers between devices  430 us (67%)
  matrix products  69.6 us (11%)
  local copies, waits for them, and re-layouts  45.7 us (7%)
  blocking collectives  40.8 us (6%)
  starting transfers between devices  21.7 us (3%)
  between operations  14.4 us (2%)
  other arithmetic  11.9 us (2%)
    psum x1, waiting for transfers between devices, per_device(): last_rows = lax.psum(board, ('seq', 'exp')).astype(jnp.float32)  117 us
    all_to_all x1, waiting for transfers between devices, per_device(): lax.all_to_all(outgoing, ('seq', 'exp'), split_axis=0, concat_axis=0, til...  93.3 us
    all_to_all x1, waiting for transfers between devices, per_device(): lax.all_to_all(part_sum.astype(jnp.bfloat16).reshape(arrived_shape), ('se...  93 us
    all_gather x1, waiting for transfers between devices, per_device(): own_weight = lax.all_gather(own_half, 'seq', axis=0, tiled=True)  64.4 us
    all_gather x1, waiting for transfers between devices, per_device(): lax.all_gather(normed, 'seq', axis=0, tiled=True)  58 us
    unnamed x1, blocking collectives  40.8 us
    dot_general x2, matrix products, share_part(): jnp.einsum('rd,gfd->rgf', flat_rows, pair, preferred_element_type=jnp.flo...  17.8 us
  transfers between devices with their start and end apart: 15, of which 7 were waited for; matrix products, arithmetic and copies ran while one was open for 12% of the time, Pallas kernels for 0%

profile of v1, /device:TPU:0, one launch (start us, length us, event | category | flops | bytes accessed | tf_op | source)
XLA Modules:
  0.0 636.2 jit_solution(1930093998321858173)
XLA Ops:
  7.2 1.3 fusion.48
  8.6 2.1 fusion.50
  10.7 0.8 constant_dynamic-slice_fusion.2
  12.2 8.0 %reshape.276 = bf16[2048,768]{1,0:T(8,128)(2,1)} reshape(bf16[2048,3,2,128]{3,2,1,0:T(2,128)(2,1)} %param.19) | data formatting | bytes 6291456 | tf_op jit(solution)/shard_map/reshape | solution.py:101
  20.3 4.7 copy.43
  25.0 1.7 reduce-window.11
  27.9 1.0 multiply_cosine_fusion
  28.9 58.0 %all-gather.5.cloned.1.call-done = bf16[1024,2048]{1,0:T(8,128)(2,1)} async-done(((bf16[128,2048]{1,0:T(8,128)(2,1)}), bf16[1024,2048]{1,0:T(8,128)(2,1)}) %all-gather.5.cloned.1.call-update) | async-done | bytes 4194320 | tf_op jit(solution)/shard_map/all_gather | solution.py:103
  86.9 6.2 fusion.31
  93.6 1.2 copy-done.4
  95.2 1.4 fusion.51
  96.9 64.4 %all-gather.7.cloned.1.call-done = bf16[16,64,2048]{2,1,0:T(8,128)(2,1)} async-done(((bf16[2,64,2048]{2,1,0:T(8,128)(2,1)}), bf16[16,64,2048]{2,1,0:T(8,128)(2,1)}) %all-gather.7.cloned.1.call-update) | async-done | bytes 4194320 | tf_op jit(solution)/shard_map/all_gather | solution.py:146
  161.3 18.0 %while.24 = (s32[]{:T(128)}, bf16[2,512,2,128]{3,2,1,0:T(2,128)(2,1)S(1)}, s32[2]{0:T(128)S(1)}, s32[1024]{0:T(1024)S(1)}, bf16[1024,2,128]{0,2,1:T(8,128)(2,1)S...) while((s32[]{:T(128)}, ...), condition=%wide.region_7.8_spmd.clone, body=%wide.region_4.7_spmd.clone.sunk | while | flops 544867840 | bytes 11557047 | solution.py:133
  163.2 3.7 fusion.118
  166.9 2.9 fusion.119
  172.1 3.7 fusion.118
  175.9 2.9 fusion.119
  180.3 0.8 collective-permute-start.1
  181.1 2.1 collective-permute-start.2
  183.3 1.6 collective-permute-start.3
  184.8 1.3 collective-permute-start.4
  186.2 1.6 collective-permute-start.5
  187.8 3.2 collective-permute-start.6
  191.1 2.4 collective-permute-done.3
  193.4 2.0 collective-permute-done.4
  196.3 2.9 convolution_bitcast_fusion.1
  199.3 3.1 multiply_reduce_fusion
  202.4 3.0 convolution_convert_fusion
  205.4 5.8 reshape.278
  211.2 5.6 all-to-all-start
  217.4 93.3 %all-to-all-done = bf16[32,28,2048]{2,1,0:T(8,128)(2,1)} async-done(((bf16[32,28,2048]{2,1,0:T(8,128)(2,1)}), bf16[32,28,2048]{2,1,0:T(8,128)(2,1)}, u32[]{:S(2)}, u32[]{:S(2)}) %all-to-all-start) | async-done | bytes 3670048 | tf_op jit(solution)/shard_map/all_to_all | solution.py:183
  310.7 5.9 reshape.306
  316.6 9.4 %fusion.77 = f32[896,2,704]{0,2,1:T(8,128)S(1)} fusion(bf16[896,2048,1]{1,0,2:T(8,128)(2,1)} %reshape.306, bf16[1,2,704,2048]{3,2,1,0:T(8,128)(2,1)} %param.24), kind=kOutput, calls=%fused_computation.146 | convolution fusion | flops 5167382528 | bytes 14483456 | tf_op jit(solution)/shard_map/rd,gfd->rgf/dot_general | solution.py:188
  326.1 3.4 fusion.44
  329.5 8.4 %fusion.89 = f32[896,2,704]{0,2,1:T(8,128)S(1)} fusion(bf16[896,2048,1]{1,0,2:T(8,128)(2,1)S(1)} %copy-done.3, bf16[2,704,2048]{2,1,0:T(8,128)(2,1)} %collective-permute-done.8), kind=kOutput, calls=%fused_computation.153 | convolution fusion | flops 5167382528 | bytes 14483456 | tf_op jit(solution)/shard_map/rd,gfd->rgf/dot_general | solution.py:188
  337.9 6.9 %add_convert_fusion = bf16[896,2048]{1,0:T(8,128)(2,1)} fusion(bf16[896,2048]{1,0:T(8,128)(2,1)S(1)} %fusion.44, bf16[704,2048]{1,0:T(8,128)(2,1)} %collective-permute-done.9, f32[896,2,704]{0,2,1:T(8,128)S(1)} %fusion.89), kind=kOutput, calls=%fused_computation.32 | convolution fusion | flops 2596651008 | bytes 15269888 | tf_op jit(solution)/shard_map/dot_general | solution.py:190
  344.8 5.8 reshape.280
  350.6 4.1 all-to-all-start.1
  355.6 93.0 %all-to-all-done.1 = bf16[32,28,2048]{2,1,0:T(8,128)(2,1)} async-done(((bf16[32,28,2048]{2,1,0:T(8,128)(2,1)}), bf16[32,28,2048]{2,1,0:T(8,128)(2,1)}, u32[]{:S(2)}, u32[]{:S(2)}) %all-to-all-start.1) | async-done | bytes 3670048 | tf_op jit(solution)/shard_map/all_to_all | solution.py:194
  448.6 5.8 reshape.281
  454.4 3.9 fusion.40
  458.6 0.6 copy-done.6
  459.3 117.0 %all-reduce.5.cloned.1.call-done = bf16[16,2048]{1,0:T(8,128)(2,1)} async-done(((bf16[16,2048]{1,0:T(8,128)(2,1)}), bf16[16,2048]{1,0:T(8,128)(2,1)}) %all-reduce.5.cloned.1.call-update) | async-done | bytes 65552 | tf_op jit(solution)/shard_map/psum | solution.py:215
  576.3 1.0 fusion.54
  577.3 8.5 %fusion.88 = (f32[16]{0:T(128)S(1)}, f32[16,3200]{1,0:T(8,128)S(1)}) fusion(bf16[3200,2048]{1,0:T(8,128)(2,1)} %param.27, bf16[16,2048]{1,0:T(8,128)(2,1)} %all-reduce.5.cloned.1.call-done, f32[2048]{0:T(1024)S(1)} %copy-done.10, f32[16]{0:T(128)S(1)} %add_rsqrt_fusion), kind=kOutput, calls=%fused_computation.152 | convolution fusion | flops 209897456 | bytes 13385856 | tf_op jit(solution)/shard_map/dot_general | solution.py:217
  586.4 40.8 %all-reduce.2 = (f32[512]{0:T(512)S(1)}, f32[512]{0:T(512)S(1)}) all-reduce(f32[512]{0:T(512)S(1)} %dynamic-update-slice, f32[512]{0:T(512)S(1)} %dynamic-update-slice.1), channel_id=2, replica_groups=mesh['seq'=8,'exp'=4] {'seq','exp'}, use_global_device_ids=true, to_apply=%add | all-reduce | flops 1024 | bytes 8192
  627.6 1.3 while.23
  628.9 0.8 broadcast_subtract_fusion
  (145 shorter events, 11.6 us)
Async XLA Ops:
  7.2 3.5 copy-start
  7.2 4.5 copy-start.9
  7.2 4.8 copy-start.12
  7.2 79.7 %all-gather.5.cloned.1.call-start = ((), (), s32[]{:S(2)}) async-start(), calls=%async_computation.2 | async-start | bytes 4718592 | tf_op jit(solution)/shard_map/all_gather | solution.py:103
  10.6 150.7 %all-gather.7.cloned.1.call-start = ((), (), s32[]{:S(2)}) async-start(), calls=%async_computation.3 | async-start | bytes 4718592 | tf_op jit(solution)/shard_map/all_gather | solution.py:146
  93.1 1.7 copy-start.4
  161.3 38.0 %collective-permute-start.7 = (bf16[16,64,2048]{2,1,0:T(8,128)(2,1)}, bf16[16,64,2048]{2,1,0:T(8,128)(2,1)}, u32[]{:S(2)}, u32[]{:S(2)}) collective-permute-start(bf16[16,64,2048]{2,1,0:T(8,128)(2,1)} %all-gather.7.cloned.1.call-done), channel_id=1, source_target_pairs={{0,1},{1,0},{2,3},{3,2},{4,5},{5,4},{6,7},{7,6},{8,9},{9,8},{10,11... | collective-permute-start | bytes 12582920 | tf_op jit(solution)/shard_map/ppermute | solution.py:63
  179.7 5.1 collective-permute-start
  180.3 5.9 collective-permute-start.1
  181.1 6.7 %collective-permute-start.2 = (bf16[128,256]{1,0:T(8,128)(2,1)S(1)}, bf16[128,256]{1,0:T(8,128)(2,1)S(1)}, u32[]{:S(2)}, u32[]{:S(2)}) collective-permute-start(bf16[128,256]{1,0:T(8,128)(2,1)S(1)} %get-tuple-element.161), channel_id=1, source_target_pairs={{0,12},{4,8},{8,4},{12,0},{16,28},{20,24},{24,20},{28,16},{1,13},{... | collective-permute-start | bytes 196616 | tf_op jit(solution)/shard_map/ppermute | solution.py:140
  183.3 10.2 %collective-permute-start.3 = (bf16[128,256]{1,0:T(8,128)(2,1)S(1)}, bf16[128,256]{1,0:T(8,128)(2,1)S(1)}, u32[]{:S(2)}, u32[]{:S(2)}) collective-permute-start(bf16[128,256]{1,0:T(8,128)(2,1)S(1)} %get-tuple-element.160), channel_id=1, source_target_pairs={{0,16},{4,20},{8,24},{12,28},{16,0},{20,4},{24,8},{28,12},{1,17},{... | collective-permute-start | bytes 196616 | tf_op jit(solution)/shard_map/ppermute | solution.py:140
  184.8 10.6 %collective-permute-start.4 = (bf16[128,256]{1,0:T(8,128)(2,1)S(1)}, bf16[128,256]{1,0:T(8,128)(2,1)S(1)}, u32[]{:S(2)}, u32[]{:S(2)}) collective-permute-start(bf16[128,256]{1,0:T(8,128)(2,1)S(1)} %get-tuple-element.159), channel_id=1, source_target_pairs={{0,20},{4,16},{8,28},{12,24},{16,4},{20,0},{24,12},{28,8},{1,21},{... | collective-permute-start | bytes 196616 | tf_op jit(solution)/shard_map/ppermute | solution.py:140
  186.2 9.2 %collective-permute-start.5 = (bf16[128,256]{1,0:T(8,128)(2,1)S(1)}, bf16[128,256]{1,0:T(8,128)(2,1)S(1)}, u32[]{:S(2)}, u32[]{:S(2)}) collective-permute-start(bf16[128,256]{1,0:T(8,128)(2,1)S(1)} %get-tuple-element.158), channel_id=1, source_target_pairs={{0,24},{4,28},{8,16},{12,20},{16,8},{20,12},{24,0},{28,4},{1,25},{... | collective-permute-start | bytes 196616 | tf_op jit(solution)/shard_map/ppermute | solution.py:140
  187.8 7.6 %collective-permute-start.6 = (bf16[128,256]{1,0:T(8,128)(2,1)S(1)}, bf16[128,256]{1,0:T(8,128)(2,1)S(1)}, u32[]{:S(2)}, u32[]{:S(2)}) collective-permute-start(bf16[128,256]{1,0:T(8,128)(2,1)S(1)} %get-tuple-element.157), channel_id=1, source_target_pairs={{0,28},{4,24},{8,20},{12,16},{16,12},{20,8},{24,4},{28,0},{1,29},{... | collective-permute-start | bytes 196616 | tf_op jit(solution)/shard_map/ppermute | solution.py:140
  195.5 3.8 copy-start.2
  199.3 3.1 copy-start.8
  211.2 99.5 %all-to-all-start = ((bf16[32,28,2048]{2,1,0:T(8,128)(2,1)}), bf16[32,28,2048]{2,1,0:T(8,128)(2,1)}, u32[]{:S(2)}, u32[]{:S(2)}) async-start(bf16[32,28,2048]{2,1,0:T(8,128)(2,1)} %reshape.278), calls=%async_computation | async-start | bytes 8388608 | tf_op jit(solution)/shard_map/all_to_all | solution.py:183
  216.8 112.7 %collective-permute-start.8 = (bf16[2,704,2048]{2,1,0:T(8,128)(2,1)}, bf16[2,704,2048]{2,1,0:T(8,128)(2,1)}, u32[]{:S(2)}, u32[]{:S(2)}) collective-permute-start(bf16[2,704,2048]{2,1,0:T(8,128)(2,1)} %bitcast.173), channel_id=1, source_target_pairs={{0,1},{1,0},{2,3},{3,2},{4,5},{5,4},{6,7},{7,6},{8,9},{9,8},{10,11... | collective-permute-start | bytes 17301512 | tf_op jit(solution)/shard_map/ppermute | solution.py:63
  217.1 120.9 %collective-permute-start.9 = (bf16[704,2048]{1,0:T(8,128)(2,1)}, bf16[704,2048]{1,0:T(8,128)(2,1)}, u32[]{:S(2)}, u32[]{:S(2)}) collective-permute-start(bf16[704,2048]{1,0:T(8,128)(2,1)} %bitcast.174), channel_id=1, source_target_pairs={{0,1},{1,0},{2,3},{3,2},{4,5},{5,4},{6,7},{7,6},{8,9},{9,8},{10,11... | collective-permute-start | bytes 8650760 | tf_op jit(solution)/shard_map/ppermute | solution.py:63
  316.6 9.4 %copy-start.11 = (bf16[1,704,2048]{2,1,0:T(8,128)(2,1)S(1)}, bf16[1,704,2048]{2,1,0:T(8,128)(2,1)}, u32[]{:S(2)}) copy-start(bf16[1,704,2048]{2,1,0:T(8,128)(2,1)} %param.25) | copy-start | bytes 8650756
  326.1 3.4 copy-start.3
  350.6 4.2 copy-start.7
  350.6 98.0 %all-to-all-start.1 = ((bf16[32,28,2048]{2,1,0:T(8,128)(2,1)}), bf16[32,28,2048]{2,1,0:T(8,128)(2,1)}, u32[]{:S(2)}, u32[]{:S(2)}) async-start(bf16[32,28,2048]{2,1,0:T(8,128)(2,1)} %reshape.280), calls=%async_computation.1 | async-start | bytes 8388608 | tf_op jit(solution)/shard_map/all_to_all | solution.py:194
  354.7 221.6 %all-reduce.5.cloned.1.call-start = ((), (), s32[]{:S(2)}) async-start(), calls=%async_computation.4 | async-start | bytes 131072 | tf_op jit(solution)/shard_map/psum | solution.py:215
  454.4 122.8 %copy-start.10 = (f32[2048]{0:T(1024)S(1)}, f32[2048]{0:T(1024)}, u32[]{:S(2)}) copy-start(f32[2048]{0:T(1024)} %param.26) | copy-start | bytes 24580
  458.3 127.4 %copy-start.5 = (bf16[128,2048]{1,0:T(8,128)(2,1)}, bf16[128,2048]{1,0:T(8,128)(2,1)S(1)}, u32[]{:S(2)}) copy-start(bf16[128,2048]{1,0:T(8,128)(2,1)S(1)} %fusion.40) | copy-start | bytes 1572868
  458.6 0.6 copy-start.6
  577.3 52.4 %copy-start.1 = (bf16[2,128,2048]{2,1,0:T(8,128)(2,1)S(1)}, bf16[2,128,2048]{2,1,0:T(8,128)(2,1)}, u32[]{:S(2)}) copy-start(bf16[2,128,2048]{2,1,0:T(8,128)(2,1)} %param.20) | copy-start | bytes 3145732
Sparse Core Ops, SparseCore 0:
  10.8 76.0 all-gather.4
  89.6 71.6 all-gather.6
  459.4 116.8 all-reduce.4
